TPU v7x, 128 devices: a whole 4x4x4 slice. The times are simulated.
128 devices in a mesh: node: 8 (over x, core), dev: 16 (over z, y).
Axes of the slice: x: 4, y: 4, z: 4, core: 2. Of those that a mesh axis runs over, the one named last changes fastest.
Arguments:
- tokens: bfloat16 [32768, 7168], P(('node', 'dev')), may hold values from -6 to 6
- grad_out: bfloat16 [32768, 7168], P(('node', 'dev')), may hold values from -1.796875 to 1.796875
- router_gates: bfloat16 [32768, 8], P(('node', 'dev')), may hold values from 0.049804688 to 1
- expert_ids: int32 [32768, 8], P(('node', 'dev')), may hold values from 0 to 255, as said below
- slot_plan: int32 [256, 2], replicated, may hold values from 0 to 16, as said below
- w_gate: bfloat16 [8, 7168, 2048], P(None, 'dev', 'node'), may hold values from -0.0625 to 0.0625
- w_up: bfloat16 [8, 7168, 2048], P(None, 'dev', 'node'), may hold values from -0.0625 to 0.0625
- w_down: bfloat16 [8, 2048, 7168], P(None, 'node', 'dev'), may hold values from -0.125 to 0.125
Outputs:
- grad_tokens: bfloat16 [32768, 7168], P(('node', 'dev'))
- grad_gates: float32 [32768, 8], P(('node', 'dev'))
- grad_w_gate: bfloat16 [8, 7168, 2048], P(None, 'dev', 'node')
- grad_w_up: bfloat16 [8, 7168, 2048], P(None, 'dev', 'node')
- grad_w_down: bfloat16 [8, 2048, 7168], P(None, 'node', 'dev')
Inputs may be any that keep to these rules, and one draw needn't show every extreme that they name: `expert_ids`: each token names 8 different experts. Within one block of 256 tokens (the tokens of one device), at most 4 pairs name any one expert that has slots, and in every draw one expert that has slots is named exactly 2 * 2 times in every block. `slot_plan`: exactly 8 rows hold slots: each such row holds two different slots, and every slot 0 .. 15 stands in exactly one row. Every entry of the other rows equals 16.
All inputs are finite; a program needn't handle non-finite values.
Results may differ from a plain program's by a relative error of at most 0.0059.
Values may be sent and summed in bfloat16 or wider, within the bound.
No kernel may reach another device: no remote copies, remote signals or barrier semaphores. Data moves between devices by JAX's collectives and lax.ppermute only.
A program may use at most 128 MiB of HBM per device.

v0:
```python
import jax
import jax.numpy as jnp
from jax import lax
from jax.sharding import PartitionSpec as P

EXPERTS = 256
TOP = 8
CAP = 2


def expert_pass(pieces, slot_gate, slot_up, slot_down):
    x_piece, dy_piece, gate_piece = pieces
    lead_count = x_piece.shape[0]
    slot_count = slot_down.shape[0]
    model_width = x_piece.shape[-1]
    x_rows = x_piece.reshape(-1, model_width)
    dy_split = dy_piece.reshape(-1, slot_count, model_width // slot_count)
    gate_rows = gate_piece.reshape(-1, 1).astype(jnp.float32)
    gate_pre = jnp.dot(x_rows, slot_gate, preferred_element_type=jnp.float32)
    up_pre = jnp.dot(x_rows, slot_up, preferred_element_type=jnp.float32)
    back_proj = jnp.einsum("rsk,shk->rh", dy_split, slot_down, preferred_element_type=jnp.float32)
    sigmoid_gate = jax.nn.sigmoid(gate_pre)
    active = gate_pre * sigmoid_gate
    hidden = active * up_pre
    scaled_back = gate_rows * back_proj
    d_gate = (scaled_back * up_pre * sigmoid_gate * (1.0 + gate_pre * (1.0 - sigmoid_gate))).astype(
        jnp.bfloat16
    )
    d_up = (scaled_back * active).astype(jnp.bfloat16)
    scaled_hidden = (gate_rows * hidden).astype(jnp.bfloat16)
    gate_terms = jnp.sum(back_proj * hidden, axis=-1)
    row_terms = jnp.einsum("rh,dh->rd", d_gate, slot_gate, preferred_element_type=jnp.float32)
    row_terms = row_terms + jnp.einsum(
        "rh,dh->rd", d_up, slot_up, preferred_element_type=jnp.float32
    )
    acc_gate = jnp.einsum("rd,rh->dh", x_rows, d_gate, preferred_element_type=jnp.float32)
    acc_up = jnp.einsum("rd,rh->dh", x_rows, d_up, preferred_element_type=jnp.float32)
    acc_down = jnp.einsum(
        "rsk,rh->shk", dy_split, scaled_hidden, preferred_element_type=jnp.float32
    )
    row_acc = row_terms.reshape(lead_count, slot_count, -1, model_width)
    gate_acc = gate_terms.reshape(lead_count, slot_count, -1)
    return (acc_gate, acc_up, acc_down, row_acc, gate_acc)


def local(tokens, grad_out, router_gates, expert_ids, slot_plan, w_gate, w_up, w_down):
    slot_count = lax.axis_size("dev")
    tok_rows, model_width = tokens.shape
    hidden_width = w_gate.shape[2]
    round_total = w_gate.shape[0]
    pair_total = tok_rows * TOP
    expert_match = expert_ids[:, :, None] == jnp.arange(EXPERTS, dtype=jnp.int32)
    first_slot = jnp.sum(jnp.where(expert_match, slot_plan[:, 0], 0), axis=-1).reshape(pair_total)
    second_slot = jnp.sum(jnp.where(expert_match, slot_plan[:, 1], 0), axis=-1).reshape(pair_total)
    is_live = first_slot < slot_count
    first_hot = (first_slot[:, None] == jnp.arange(slot_count, dtype=jnp.int32)[None, :]).astype(
        jnp.int32
    )
    pair_order = jnp.sum(first_hot * (jnp.cumsum(first_hot, axis=0) - 1), axis=-1)
    pair_slot = jnp.where(pair_order % 2 == 0, first_slot, second_slot)
    target_row = pair_slot * CAP + pair_order // 2
    position_ids = jnp.arange(slot_count * CAP, dtype=jnp.int32)
    chooser = (is_live[None, :] & (target_row[None, :] == position_ids[:, None])).astype(
        jnp.float32
    )
    pick_rows = jnp.sum(chooser.reshape(slot_count * CAP, tok_rows, TOP), axis=-1)
    pick_half = pick_rows.astype(jnp.bfloat16)
    x_send = (
        jnp.dot(pick_half, tokens, preferred_element_type=jnp.float32)
        .astype(jnp.bfloat16)
        .reshape(slot_count, CAP, model_width)
    )
    dy_send = (
        jnp.dot(pick_half, grad_out, preferred_element_type=jnp.float32)
        .astype(jnp.bfloat16)
        .reshape(slot_count, CAP, model_width)
    )
    flat_gates = router_gates.reshape(pair_total).astype(jnp.float32)
    gate_send = (
        jnp.dot(chooser, flat_gates, precision=lax.Precision.HIGHEST)
        .astype(jnp.bfloat16)
        .reshape(slot_count, CAP)
    )
    in_round = (slot_plan[:, 0] < slot_count).astype(jnp.int32)
    expert_rank = jnp.cumsum(in_round) - 1
    holder = jnp.any(slot_plan[:, :, None] == jnp.arange(slot_count, dtype=jnp.int32), axis=1)
    slot_rank = jnp.sum(jnp.where(holder, expert_rank[:, None], 0), axis=0)
    grouping = (slot_rank[None, :] == jnp.arange(round_total, dtype=jnp.int32)[:, None]).astype(
        jnp.bfloat16
    )
    copy_gate = jnp.take(w_gate, slot_rank, axis=0)
    copy_up = jnp.take(w_up, slot_rank, axis=0)
    copy_down = jnp.take(w_down, slot_rank, axis=0)
    slot_gate, slot_up, slot_down = (
        lax.all_to_all(copy_gate, "dev", split_axis=0, concat_axis=0, tiled=True),
        lax.all_to_all(copy_up, "dev", split_axis=0, concat_axis=0, tiled=True),
        lax.all_to_all(copy_down, "dev", split_axis=0, concat_axis=0, tiled=True),
    )
    slot_gate = slot_gate.reshape(model_width, hidden_width)
    slot_up = slot_up.reshape(model_width, hidden_width)
    got_x, got_dy, got_gate = (
        lax.all_to_all(x_send, "dev", split_axis=0, concat_axis=0, tiled=True),
        lax.all_to_all(dy_send, "dev", split_axis=0, concat_axis=0, tiled=True),
        lax.all_to_all(gate_send, "dev", split_axis=0, concat_axis=0, tiled=True),
    )
    totals = expert_pass(
        (
            lax.all_gather(got_x[None], "node", axis=0, tiled=True),
            lax.all_gather(got_dy[None], "node", axis=0, tiled=True),
            lax.all_gather(got_gate[None], "node", axis=0, tiled=True),
        ),
        slot_gate,
        slot_up,
        slot_down,
    )
    acc_gate, acc_up, acc_down, row_acc, gate_acc = totals
    summed_rows, summed_gates = (
        lax.psum_scatter(row_acc, "node", scatter_dimension=0, tiled=True),
        lax.psum_scatter(gate_acc, "node", scatter_dimension=0, tiled=True),
    )
    back_rows, back_gates = (
        lax.all_to_all(summed_rows, "dev", split_axis=1, concat_axis=1, tiled=True),
        lax.all_to_all(summed_gates, "dev", split_axis=1, concat_axis=1, tiled=True),
    )
    grad_tokens = jnp.einsum(
        "qt,qd->td",
        pick_rows,
        back_rows.reshape(slot_count * CAP, model_width),
        precision=lax.Precision.HIGHEST,
    ).astype(jnp.bfloat16)
    grad_gates = jnp.dot(
        back_gates.reshape(slot_count * CAP), chooser, precision=lax.Precision.HIGHEST
    ).reshape(tok_rows, TOP)
    send_gate = acc_gate.astype(jnp.bfloat16).reshape(
        slot_count, model_width // slot_count, hidden_width
    )
    send_up = acc_up.astype(jnp.bfloat16).reshape(
        slot_count, model_width // slot_count, hidden_width
    )
    send_down = acc_down.astype(jnp.bfloat16)
    got_wgate, got_wup, got_wdown = (
        lax.all_to_all(send_gate, "dev", split_axis=0, concat_axis=0, tiled=True),
        lax.all_to_all(send_up, "dev", split_axis=0, concat_axis=0, tiled=True),
        lax.all_to_all(send_down, "dev", split_axis=0, concat_axis=0, tiled=True),
    )
    grad_w_gate = jnp.einsum(
        "js,sdh->jdh", grouping, got_wgate, preferred_element_type=jnp.float32
    ).astype(jnp.bfloat16)
    grad_w_up = jnp.einsum(
        "js,sdh->jdh", grouping, got_wup, preferred_element_type=jnp.float32
    ).astype(jnp.bfloat16)
    grad_w_down = jnp.einsum(
        "js,shk->jhk", grouping, got_wdown, preferred_element_type=jnp.float32
    ).astype(jnp.bfloat16)
    return (grad_tokens, grad_gates, grad_w_gate, grad_w_up, grad_w_down)


def solution(mesh):
    return jax.shard_map(
        local,
        mesh=mesh,
        in_specs=(
            P(("node", "dev"), None),
            P(("node", "dev"), None),
            P(("node", "dev"), None),
            P(("node", "dev"), None),
            P(),
            P(None, "dev", "node"),
            P(None, "dev", "node"),
            P(None, "node", "dev"),
        ),
        out_specs=(
            P(("node", "dev"), None),
            P(("node", "dev"), None),
            P(None, "dev", "node"),
            P(None, "dev", "node"),
            P(None, "node", "dev"),
        ),
        check_vma=False,
    )
```

profile of v0, /device:TPU:14, one launch (start us, length us, event | category | flops | bytes accessed | tf_op | source)
XLA Modules:
  0.0 506.6 jit_solution(3346200505427443808)
XLA Ops:
  8.9 9.2 %select_reduce_fusion = (s32[256,8]{1,0:T(8,128)S(1)}, s32[256,8]{1,0:T(8,128)S(1)}) fusion(s32[256]{0:T(256)S(1)} %bitcast.78, s32[256,8]{1,0:T(8,128)S(1)} %copy.90, s32[256]{0:T(256)S(1)} %bitcast.77), kind=kLoop, calls=%fused_computation.21 | loop fusion | flops 2617344 | bytes 26624 | tf_op jit(solution)/shard_map/reduce_sum | solution.py:54
  27.2 17.7 %all_to_all.60 = bf16[16,2,7168]{2,1,0:T(2,128)(2,1)} all-to-all(bf16[16,2,7168]{2,1,0:T(2,128)(2,1)S(1)} %reshape.235), channel_id=1, replica_groups=mesh['node'=8,'dev'=16] {'dev'}, dimensions={0} | all-to-all | bytes 917504 | tf_op jit(solution)/shard_map/all_to_all | solution.py:102
  62.3 7.3 %all-to-all-start.1 = ((bf16[16,2,7168]{2,1,0:T(2,128)(2,1)}), bf16[16,2,7168]{2,1,0:T(2,128)(2,1)S(1)}, u32[]{:S(2)}, u32[]{:S(2)}) async-start(bf16[16,2,7168]{2,1,0:T(2,128)(2,1)} %reshape.232), calls=%async_computation.1 | async-start | bytes 917504 | tf_op jit(solution)/shard_map/all_to_all | solution.py:103
  85.4 44.8 %all-to-all-done.5 = bf16[16,448,256]{2,1,0:T(8,128)(2,1)} async-done(((bf16[16,448,256]{2,1,0:T(8,128)(2,1)}), bf16[16,448,256]{2,1,0:T(8,128)(2,1)}, u32[]{:S(2)}, u32[]{:S(2)}) %all-to-all-start.5) | async-done | bytes 3670048 | tf_op jit(solution)/shard_map/all_to_all | solution.py:95
  130.2 9.0 %all-to-all-start.4 = ((bf16[16,448,256]{2,1,0:T(8,128)(2,1)}), bf16[16,448,256]{2,1,0:T(8,128)(2,1)}, u32[]{:S(2)}, u32[]{:S(2)}) async-start(bf16[16,448,256]{2,1,0:T(8,128)(2,1)} %get-tuple-element.43), calls=%async_computation.4 | async-start | bytes 7340032 | tf_op jit(solution)/shard_map/all_to_all | solution.py:96
  146.2 38.6 %all-to-all-done.4 = bf16[16,448,256]{2,1,0:T(8,128)(2,1)} async-done(((bf16[16,448,256]{2,1,0:T(8,128)(2,1)}), bf16[16,448,256]{2,1,0:T(8,128)(2,1)}, u32[]{:S(2)}, u32[]{:S(2)}) %all-to-all-start.4) | async-done | bytes 3670048 | tf_op jit(solution)/shard_map/all_to_all | solution.py:96
  184.7 8.8 %all-to-all-start.2 = ((bf16[16,256,448]{1,2,0:T(8,128)(2,1)}), bf16[16,256,448]{1,2,0:T(8,128)(2,1)}, u32[]{:S(2)}, u32[]{:S(2)}) async-start(bf16[16,256,448]{1,2,0:T(8,128)(2,1)} %broadcast_select_fusion.2), calls=%async_computation.2 | async-start | bytes 7340032 | tf_op jit(solution)/shard_map/all_to_all | solution.py:97
  193.6 13.0 %all-gather = bf16[128,1,2]{2,1,0:T(2,128)(2,1)S(1)} all-gather(bf16[16,1,2]{2,1,0:T(2,128)(2,1)S(1)} %all-to-all-done), channel_id=2, replica_groups=mesh['node'=8,'dev'=16] {'node'}, dimensions={0}, use_global_device_ids=true | all-gather | bytes 576 | tf_op jit(solution)/shard_map/all_gather | solution.py:110
  206.9 8.4 %reshape.236 = bf16[256,7168]{1,0:T(8,128)(2,1)} reshape(bf16[128,2,7168]{2,1,0:T(2,128)(2,1)} %all-gather.8.cloned.1.call-done) | data formatting | bytes 7340032 | tf_op jit(solution)/shard_map/reshape | solution.py:16
  215.3 9.6 %reshape.233 = bf16[256,16,448]{2,1,0:T(8,128)(2,1)} reshape(bf16[128,2,7168]{2,1,0:T(2,128)(2,1)} %all-gather.6.cloned.1.call-done) | data formatting | bytes 7340032 | tf_op jit(solution)/shard_map/reshape | solution.py:17
  239.1 8.3 %multiply_reduce_fusion = (f32[256]{0:T(256)S(1)}, bf16[256,256]{0,1:T(8,128)(2,1)S(1)}, bf16[256,256]{0,1:T(8,128)(2,1)S(1)}) fusion(f32[256,256]{0,1:T(8,128)S(1)} %fusion.61, f32[256,256]{0,1:T(8,128)S(1)} %fusion.62, f32[256]{0:T(256)S(1)} %reshape.245, bf16[16,256,448]{1,2,0:T(8,128)(2,1)} %all-to-all-done.2, bf16[256,16,448]{2,1,0:T(8,128)(2,1)} %reshape.233), kind=kOutput, calls=%fused_computation.32 | convolution fusion | flops 940637952 | bytes 8128512 | tf_op jit(solution)/shard_map/rsk,shk->rh/dot_general | solution.py:21
  254.5 8.3 %convolution_add_fusion = f32[256,7168]{1,0:T(8,128)} fusion(f32[256,7168]{1,0:T(8,128)} %fusion.63, bf16[256,256]{0,1:T(8,128)(2,1)S(1)} %get-tuple-element.40, bf16[7168,256]{1,0:T(8,128)(2,1)} %bitcast.9), kind=kOutput, calls=%fused_computation.3 | convolution fusion | flops 941359104 | bytes 18481152 | tf_op jit(solution)/shard_map/rh,dh->rd/dot_general | solution.py:33
  262.8 9.7 %reshape.239 = f32[8,16,2,7168]{3,2,1,0:T(2,128)} reshape(f32[256,7168]{1,0:T(8,128)} %convolution_add_fusion) | data formatting | bytes 14680064 | tf_op jit(solution)/shard_map/reshape | solution.py:41
  272.6 8.3 %copy.96 = f32[8,16,2,7168]{3,1,2,0:T(8,128)} copy(f32[8,16,2,7168]{3,2,1,0:T(2,128)} %reshape.239) | data formatting | bytes 14680064 | tf_op jit(solution)/shard_map/reshape | solution.py:41
  280.9 8.5 %copy.103 = bf16[256,16,448]{0,1,2:T(8,128)(2,1)} copy(bf16[256,16,448]{2,1,0:T(8,128)(2,1)} %reshape.233) | data formatting | bytes 7340032 | tf_op jit(solution)/shard_map/reshape | solution.py:17
  289.4 8.9 %all-to-all-start.7 = ((f32[1,16,2]{2,0,1:T(1,128)}), f32[1,16,2]{2,0,1:T(1,128)S(1)}, u32[]{:S(2)}, u32[]{:S(2)}) async-start(f32[1,16,2]{2,0,1:T(1,128)} %bitcast.76), calls=%async_computation.9 | async-start | bytes 16384 | tf_op jit(solution)/shard_map/all_to_all | solution.py:123
  304.8 7.3 %all-to-all-start.10 = ((bf16[16,256,448]{1,2,0:T(8,128)(2,1)}), bf16[16,256,448]{1,2,0:T(8,128)(2,1)}, u32[]{:S(2)}, u32[]{:S(2)}) async-start(bf16[16,256,448]{1,2,0:T(8,128)(2,1)} %copy.104), calls=%async_computation.12 | async-start | bytes 7340032 | tf_op jit(solution)/shard_map/all_to_all | solution.py:144
  317.2 39.1 %all-to-all-done.10 = bf16[16,256,448]{1,2,0:T(8,128)(2,1)} async-done(((bf16[16,256,448]{1,2,0:T(8,128)(2,1)}), bf16[16,256,448]{1,2,0:T(8,128)(2,1)}, u32[]{:S(2)}, u32[]{:S(2)}) %all-to-all-start.10) | async-done | bytes 3670048 | tf_op jit(solution)/shard_map/all_to_all | solution.py:144
  356.3 8.1 %all-to-all-start.8 = ((bf16[16,448,256]{2,1,0:T(8,128)(2,1)}), bf16[16,448,256]{2,1,0:T(8,128)(2,1)}, u32[]{:S(2)}, u32[]{:S(2)}) async-start(bf16[16,448,256]{2,1,0:T(8,128)(2,1)} %bitcast.72), calls=%async_computation.10 | async-start | bytes 7340032 | tf_op jit(solution)/shard_map/all_to_all | solution.py:142
  369.5 41.6 %all-to-all-done.8 = bf16[16,448,256]{2,1,0:T(8,128)(2,1)} async-done(((bf16[16,448,256]{2,1,0:T(8,128)(2,1)}), bf16[16,448,256]{2,1,0:T(8,128)(2,1)}, u32[]{:S(2)}, u32[]{:S(2)}) %all-to-all-start.8) | async-done | bytes 3670048 | tf_op jit(solution)/shard_map/all_to_all | solution.py:142
  411.0 9.3 %all-to-all-start.9 = ((bf16[16,448,256]{2,1,0:T(8,128)(2,1)}), bf16[16,448,256]{2,1,0:T(8,128)(2,1)}, u32[]{:S(2)}, u32[]{:S(2)}) async-start(bf16[16,448,256]{2,1,0:T(8,128)(2,1)} %bitcast.71), calls=%async_computation.11 | async-start | bytes 7340032 | tf_op jit(solution)/shard_map/all_to_all | solution.py:143
  426.3 38.1 %all-to-all-done.9 = bf16[16,448,256]{2,1,0:T(8,128)(2,1)} async-done(((bf16[16,448,256]{2,1,0:T(8,128)(2,1)}), bf16[16,448,256]{2,1,0:T(8,128)(2,1)}, u32[]{:S(2)}, u32[]{:S(2)}) %all-to-all-start.9) | async-done | bytes 3670048 | tf_op jit(solution)/shard_map/all_to_all | solution.py:143
  464.4 7.9 %all-to-all-start.6 = ((f32[1,16,2,7168]{3,2,0,1:T(2,128)}), f32[1,16,2,7168]{3,2,0,1:T(2,128)S(1)}, u32[]{:S(2)}, u32[]{:S(2)}) async-start(f32[1,16,2,7168]{3,2,0,1:T(2,128)} %copy.97), calls=%async_computation.7 | async-start | bytes 1835008 | tf_op jit(solution)/shard_map/all_to_all | solution.py:122
  491.4 8.5 %convolution_convert_fusion.2 = bf16[256,7168]{1,0:T(8,128)(2,1)} fusion(f32[32,256]{1,0:T(8,128)S(1)} %convert_reduce_fusion, f32[32,7168]{1,0:T(8,128)} %reshape.240), kind=kOutput, calls=%fused_computation.6 | convolution fusion | flops 706478080 | bytes 4620288 | tf_op jit(solution)/shard_map/qt,qd->td/dot_general | solution.py:125
  (101 shorter events, 114.1 us)
Async XLA Ops:
  7.2 44.6 %copy-start = (bf16[8,448,256]{2,1,0:T(8,128)(2,1)S(1)}, bf16[8,448,256]{2,1,0:T(8,128)(2,1)}, u32[]{:S(2)}) copy-start(bf16[8,448,256]{2,1,0:T(8,128)(2,1)} %param.16) | copy-start | bytes 5505028
  7.2 199.7 %all-gather.8.cloned.1.call-start = ((), (), s32[]{:S(2)}) async-start(), calls=%async_computation.16 | async-start | bytes 4128768 | tf_op jit(solution)/shard_map/all_gather | solution.py:108
  23.9 21.2 %copy-start.6 = (bf16[256,8]{0,1:T(8,128)(2,1)S(1)}, bf16[256,8]{0,1:T(8,128)(2,1)}, u32[]{:S(2)}) copy-start(bf16[256,8]{0,1:T(8,128)(2,1)} %param.12) | copy-start | bytes 12292
  24.0 26.9 %copy-start.5 = (s32[256,2]{0,1:T(2,128)S(1)}, s32[256,2]{0,1:T(2,128)}, u32[]{:S(2)}) copy-start(s32[256,2]{0,1:T(2,128)} %param.14) | copy-start | bytes 6148
  46.2 16.1 %all-to-all-start = ((bf16[16,1,2]{2,1,0:T(2,128)(2,1)}), bf16[16,1,2]{2,1,0:T(2,128)(2,1)S(1)}, u32[]{:S(2)}, u32[]{:S(2)}) async-start(bf16[16,1,2]{2,1,0:T(2,128)(2,1)} %all_to_all.48), calls=%async_computation | async-start | bytes 16384 | tf_op jit(solution)/shard_map/all_to_all | solution.py:104
  62.3 15.7 %all-to-all-start.1 = ((bf16[16,2,7168]{2,1,0:T(2,128)(2,1)}), bf16[16,2,7168]{2,1,0:T(2,128)(2,1)S(1)}, u32[]{:S(2)}, u32[]{:S(2)}) async-start(bf16[16,2,7168]{2,1,0:T(2,128)(2,1)} %reshape.232), calls=%async_computation.1 | async-start | bytes 917504 | tf_op jit(solution)/shard_map/all_to_all | solution.py:103
  78.0 0.8 copy-start.4
  78.8 51.4 %all-to-all-start.5 = ((bf16[16,448,256]{2,1,0:T(8,128)(2,1)}), bf16[16,448,256]{2,1,0:T(8,128)(2,1)}, u32[]{:S(2)}, u32[]{:S(2)}) async-start(bf16[16,448,256]{2,1,0:T(8,128)(2,1)} %get-tuple-element.44), calls=%async_computation.5 | async-start | bytes 7340032 | tf_op jit(solution)/shard_map/all_to_all | solution.py:95
  84.6 130.6 %all-gather.6.cloned.1.call-start = ((), (), s32[]{:S(2)}) async-start(), calls=%async_computation.15 | async-start | bytes 4128768 | tf_op jit(solution)/shard_map/all_gather | solution.py:109
  130.2 9.1 %copy-start.3 = (bf16[8,256,448]{1,2,0:T(8,128)(2,1)S(1)}, bf16[8,256,448]{1,2,0:T(8,128)(2,1)}, u32[]{:S(2)}) copy-start(bf16[8,256,448]{1,2,0:T(8,128)(2,1)} %param.17) | copy-start | bytes 5505028
  130.2 54.6 %all-to-all-start.4 = ((bf16[16,448,256]{2,1,0:T(8,128)(2,1)}), bf16[16,448,256]{2,1,0:T(8,128)(2,1)}, u32[]{:S(2)}, u32[]{:S(2)}) async-start(bf16[16,448,256]{2,1,0:T(8,128)(2,1)} %get-tuple-element.43), calls=%async_computation.4 | async-start | bytes 7340032 | tf_op jit(solution)/shard_map/all_to_all | solution.py:96
  184.7 54.4 %all-to-all-start.2 = ((bf16[16,256,448]{1,2,0:T(8,128)(2,1)}), bf16[16,256,448]{1,2,0:T(8,128)(2,1)}, u32[]{:S(2)}, u32[]{:S(2)}) async-start(bf16[16,256,448]{1,2,0:T(8,128)(2,1)} %broadcast_select_fusion.2), calls=%async_computation.2 | async-start | bytes 7340032 | tf_op jit(solution)/shard_map/all_to_all | solution.py:97
  193.5 95.9 %reduce-scatter.5.cloned.1.call-start = ((), (), s32[]{:S(2)}) async-start(), calls=%async_computation.14 | async-start | bytes 73728 | tf_op jit(solution)/shard_map/reduce_scatter | solution.py:119
  224.9 4.8 copy-start.2
  254.4 169.1 %reduce-scatter.3.cloned.1.call-start = ((), (), s32[]{:S(2)}) async-start(), calls=%async_computation.13 | async-start | bytes 8257536 | tf_op jit(solution)/shard_map/reduce_scatter | solution.py:118
  289.4 15.4 %all-to-all-start.7 = ((f32[1,16,2]{2,0,1:T(1,128)}), f32[1,16,2]{2,0,1:T(1,128)S(1)}, u32[]{:S(2)}, u32[]{:S(2)}) async-start(f32[1,16,2]{2,0,1:T(1,128)} %bitcast.76), calls=%async_computation.9 | async-start | bytes 16384 | tf_op jit(solution)/shard_map/all_to_all | solution.py:123
  304.8 51.5 %all-to-all-start.10 = ((bf16[16,256,448]{1,2,0:T(8,128)(2,1)}), bf16[16,256,448]{1,2,0:T(8,128)(2,1)}, u32[]{:S(2)}, u32[]{:S(2)}) async-start(bf16[16,256,448]{1,2,0:T(8,128)(2,1)} %copy.104), calls=%async_computation.12 | async-start | bytes 7340032 | tf_op jit(solution)/shard_map/all_to_all | solution.py:144
  356.3 54.7 %all-to-all-start.8 = ((bf16[16,448,256]{2,1,0:T(8,128)(2,1)}), bf16[16,448,256]{2,1,0:T(8,128)(2,1)}, u32[]{:S(2)}, u32[]{:S(2)}) async-start(bf16[16,448,256]{2,1,0:T(8,128)(2,1)} %bitcast.72), calls=%async_computation.10 | async-start | bytes 7340032 | tf_op jit(solution)/shard_map/all_to_all | solution.py:142
  411.0 53.4 %all-to-all-start.9 = ((bf16[16,448,256]{2,1,0:T(8,128)(2,1)}), bf16[16,448,256]{2,1,0:T(8,128)(2,1)}, u32[]{:S(2)}, u32[]{:S(2)}) async-start(bf16[16,448,256]{2,1,0:T(8,128)(2,1)} %bitcast.71), calls=%async_computation.11 | async-start | bytes 7340032 | tf_op jit(solution)/shard_map/all_to_all | solution.py:143
  464.4 25.4 %all-to-all-start.6 = ((f32[1,16,2,7168]{3,2,0,1:T(2,128)}), f32[1,16,2,7168]{3,2,0,1:T(2,128)S(1)}, u32[]{:S(2)}, u32[]{:S(2)}) async-start(f32[1,16,2,7168]{3,2,0,1:T(2,128)} %copy.97), calls=%async_computation.7 | async-start | bytes 1835008 | tf_op jit(solution)/shard_map/all_to_all | solution.py:122
  488.2 11.7 %copy-start.1 = (bf16[8,448,256]{2,1,0:T(8,128)(2,1)S(1)}, bf16[8,448,256]{2,1,0:T(8,128)(2,1)}, u32[]{:S(2)}) copy-start(bf16[8,448,256]{2,1,0:T(8,128)(2,1)} %param.16) | copy-start | bytes 5505028
Sparse Core Ops, SparseCore 0:
  45.1 26.5 all-gather.7
  87.7 29.2 all-gather.5
  254.6 30.1 reduce-scatter.4
  287.0 47.4 reduce-scatter.2
where the time goes:
time: 516 us; the launch traced here: 507 us
  waiting for transfers between devices  210 us (41%)
  starting transfers between devices  77.3 us (15%)
  local copies, waits for them, and re-layouts  74.5 us (14%)
  matrix products  72.8 us (14%)
  blocking collectives  30.7 us (6%)
  other arithmetic  27.2 us (5%)
  between operations  14.2 us (3%)
    all_to_all x1, waiting for transfers between devices, local(): lax.all_to_all(copy_gate, 'dev', split_axis=0, concat_axis=0, tiled=True)  44.8 us
    all_to_all x1, waiting for transfers between devices, local(): lax.all_to_all(send_gate, 'dev', split_axis=0, concat_axis=0, tiled=True)  41.6 us
    all_to_all x1, waiting for transfers between devices, local(): lax.all_to_all(send_down, 'dev', split_axis=0, concat_axis=0, tiled=True)  39.1 us
    all_to_all x1, waiting for transfers between devices, local(): lax.all_to_all(copy_up, 'dev', split_axis=0, concat_axis=0, tiled=True)  38.6 us
    all_to_all x1, waiting for transfers between devices, local(): lax.all_to_all(send_up, 'dev', split_axis=0, concat_axis=0, tiled=True)  38.1 us
    reshape x2, local copies, waits for them, and re-layouts, expert_pass(): dy_split = dy_piece.reshape(-1, slot_count, model_width // slot_count)  18.1 us
    reshape x2, local copies, waits for them, and re-layouts, expert_pass(): row_acc = row_terms.reshape(lead_count, slot_count, -1, model_width)  18 us
    all_to_all x1, blocking collectives, local(): lax.all_to_all(x_send, 'dev', split_axis=0, concat_axis=0, tiled=True)  17.7 us
  transfers between devices with their start and end apart: 14, of which 7 were waited for; matrix products, arithmetic and copies ran while one was open for 25% of the time, Pallas kernels for 0%

commit v1 on v0

--- a/solution.py
+++ b/solution.py
@@ -1,3 +1,4 @@
+import functools
 import jax
 import jax.numpy as jnp
 from jax import lax
@@ -6,6 +7,16 @@
 EXPERTS = 256
 TOP = 8
 CAP = 2
+
+
+def trails_process(z, peer_axis, array_axis):
+    return jnp.concatenate(
+        lax.all_to_all(jnp.stack([z] * lax.psum(1, peer_axis), axis=0), peer_axis, 0, 0),
+        axis=array_axis,
+    )
+
+
+_push_files = functools.partial(trails_process, peer_axis="node", array_axis=0)
 
 
 def expert_pass(pieces, slot_gate, slot_up, slot_down):
@@ -107,7 +118,7 @@
         (
             lax.all_gather(got_x[None], "node", axis=0, tiled=True),
             lax.all_gather(got_dy[None], "node", axis=0, tiled=True),
-            lax.all_gather(got_gate[None], "node", axis=0, tiled=True),
+            _push_files(got_gate[None]),
         ),
         slot_gate,
         slot_up,

time: 516 us -> 531 us (1.029)
  waiting for transfers between devices: 210 us -> 233 us
  blocking collectives: 30.7 us -> 17.7 us
    all_gather x1 -> x0, blocking collectives: 13 us -> none  [local(): lax.all_gather(got_gate[None], 'node', axis=0, tiled=True)]
    all_to_all x1, waiting for transfers between devices: 5.71 us -> 17 us  [local(): lax.all_to_all(copy_down, 'dev', split_axis=0, concat_axis=0, tiled=True)]
  transfers between devices with their start and end apart: 14 -> 15, of which waited for: 7 -> 8; matrix products, arithmetic and copies ran while one was open for 25% -> 25% of each run, Pallas kernels for 0% -> 0%
where the time goes in v1:
time: 531 us; the launch traced here: 521 us
  waiting for transfers between devices  233 us (44%)
  starting transfers between devices  81.6 us (15%)
  local copies, waits for them, and re-layouts  75.4 us (14%)
  matrix products  72.9 us (14%)
  other arithmetic  27 us (5%)
  blocking collectives  17.7 us (3%)
  between operations  14.2 us (3%)
    all_to_all x1, waiting for transfers between devices, local(): lax.all_to_all(copy_gate, 'dev', split_axis=0, concat_axis=0, tiled=True)  48.6 us
    all_to_all x1, waiting for transfers between devices, local(): lax.all_to_all(send_down, 'dev', split_axis=0, concat_axis=0, tiled=True)  41.6 us
    all_to_all x1, waiting for transfers between devices, local(): lax.all_to_all(send_up, 'dev', split_axis=0, concat_axis=0, tiled=True)  40.2 us
    all_to_all x1, waiting for transfers between devices, local(): lax.all_to_all(send_gate, 'dev', split_axis=0, concat_axis=0, tiled=True)  39.6 us
    all_to_all x1, waiting for transfers between devices, local(): lax.all_to_all(copy_up, 'dev', split_axis=0, concat_axis=0, tiled=True)  39.2 us
    reshape x2, local copies, waits for them, and re-layouts, expert_pass(): dy_split = dy_piece.reshape(-1, slot_count, model_width // slot_count)  18.1 us
    reshape x2, local copies, waits for them, and re-layouts, expert_pass(): row_acc = row_terms.reshape(lead_count, slot_count, -1, model_width)  18 us
    all_to_all x1, blocking collectives, local(): lax.all_to_all(x_send, 'dev', split_axis=0, concat_axis=0, tiled=True)  17.7 us
  transfers between devices with their start and end apart: 15, of which 8 were waited for; matrix products, arithmetic and copies ran while one was open for 25% of the time, Pallas kernels for 0%

profile of v1, /device:TPU:14, one launch (start us, length us, event | category | flops | bytes accessed | tf_op | source)
XLA Modules:
  0.0 521.3 jit_solution(7929755637342573438)
XLA Ops:
  8.9 9.2 %select_reduce_fusion = (s32[256,8]{1,0:T(8,128)S(1)}, s32[256,8]{1,0:T(8,128)S(1)}) fusion(s32[256]{0:T(256)S(1)} %bitcast.83, s32[256,8]{1,0:T(8,128)S(1)} %copy.79, s32[256]{0:T(256)S(1)} %bitcast.82), kind=kLoop, calls=%fused_computation.21 | loop fusion | flops 2617344 | bytes 26624 | tf_op jit(solution)/shard_map/reduce_sum | solution.py:65
  27.2 17.7 %all_to_all.65 = bf16[16,2,7168]{2,1,0:T(2,128)(2,1)} all-to-all(bf16[16,2,7168]{2,1,0:T(2,128)(2,1)S(1)} %reshape.238), channel_id=1, replica_groups=mesh['node'=8,'dev'=16] {'dev'}, dimensions={0} | all-to-all | bytes 917504 | tf_op jit(solution)/shard_map/all_to_all | solution.py:113
  75.3 7.0 %broadcast_select_fusion.1 = (bf16[16,448,256]{2,1,0:T(8,128)(2,1)}, bf16[16,448,256]{2,1,0:T(8,128)(2,1)}) fusion(bf16[16,448,256]{2,1,0:T(8,128)(2,1)} %gather_fusion.1, pred[16]{0:T(512)(128)(4,1)S(1)} %compare_and_fusion, bf16[16,448,256]{2,1,0:T(8,128)(2,1)} %gather_fusion.2), kind=kLoop, calls=%fused_computation.19 | loop fusion | flops 3670016 | bytes 14680080 | tf_op jit(solution)/shard_map/jit(_take)/select_n | solution.py:103
  92.5 48.6 %all-to-all-done.6 = bf16[16,448,256]{2,1,0:T(8,128)(2,1)} async-done(((bf16[16,448,256]{2,1,0:T(8,128)(2,1)}), bf16[16,448,256]{2,1,0:T(8,128)(2,1)}, u32[]{:S(2)}, u32[]{:S(2)}) %all-to-all-start.6) | async-done | bytes 3670048 | tf_op jit(solution)/shard_map/all_to_all | solution.py:106
  141.1 9.1 %all-to-all-start.5 = ((bf16[16,448,256]{2,1,0:T(8,128)(2,1)}), bf16[16,448,256]{2,1,0:T(8,128)(2,1)}, u32[]{:S(2)}, u32[]{:S(2)}) async-start(bf16[16,448,256]{2,1,0:T(8,128)(2,1)} %get-tuple-element.38), calls=%async_computation.5 | async-start | bytes 7340032 | tf_op jit(solution)/shard_map/all_to_all | solution.py:107
  157.2 39.2 %all-to-all-done.5 = bf16[16,448,256]{2,1,0:T(8,128)(2,1)} async-done(((bf16[16,448,256]{2,1,0:T(8,128)(2,1)}), bf16[16,448,256]{2,1,0:T(8,128)(2,1)}, u32[]{:S(2)}, u32[]{:S(2)}) %all-to-all-start.5) | async-done | bytes 3670048 | tf_op jit(solution)/shard_map/all_to_all | solution.py:107
  196.4 9.6 %all-to-all-start.3 = ((bf16[16,256,448]{1,2,0:T(8,128)(2,1)}), bf16[16,256,448]{1,2,0:T(8,128)(2,1)}, u32[]{:S(2)}, u32[]{:S(2)}) async-start(bf16[16,256,448]{1,2,0:T(8,128)(2,1)} %broadcast_select_fusion.2), calls=%async_computation.3 | async-start | bytes 7340032 | tf_op jit(solution)/shard_map/all_to_all | solution.py:108
  206.6 8.4 %reshape.239 = bf16[256,7168]{1,0:T(8,128)(2,1)} reshape(bf16[128,2,7168]{2,1,0:T(2,128)(2,1)} %all-gather.7.cloned.1.call-done) | data formatting | bytes 7340032 | tf_op jit(solution)/shard_map/reshape | solution.py:27
  215.0 9.6 %reshape.236 = bf16[256,16,448]{2,1,0:T(8,128)(2,1)} reshape(bf16[128,2,7168]{2,1,0:T(2,128)(2,1)} %all-gather.5.cloned.1.call-done) | data formatting | bytes 7340032 | tf_op jit(solution)/shard_map/reshape | solution.py:28
  233.1 17.0 %all-to-all-done.3 = bf16[16,256,448]{1,2,0:T(8,128)(2,1)} async-done(((bf16[16,256,448]{1,2,0:T(8,128)(2,1)}), bf16[16,256,448]{1,2,0:T(8,128)(2,1)}, u32[]{:S(2)}, u32[]{:S(2)}) %all-to-all-start.3) | async-done | bytes 3670048 | tf_op jit(solution)/shard_map/all_to_all | solution.py:108
  250.1 8.3 %multiply_reduce_fusion = (f32[256]{0:T(256)S(1)}, bf16[256,256]{0,1:T(8,128)(2,1)S(1)}, bf16[256,256]{0,1:T(8,128)(2,1)S(1)}) fusion(f32[256,256]{0,1:T(8,128)S(1)} %fusion.61, f32[256,256]{0,1:T(8,128)S(1)} %fusion.62, f32[256]{0:T(256)S(1)} %reshape.248, bf16[16,256,448]{1,2,0:T(8,128)(2,1)} %all-to-all-done.3, bf16[256,16,448]{2,1,0:T(8,128)(2,1)} %reshape.236), kind=kOutput, calls=%fused_computation.32 | convolution fusion | flops 940637952 | bytes 8128512 | tf_op jit(solution)/shard_map/rsk,shk->rh/dot_general | solution.py:32
  265.5 8.4 %convolution_add_fusion = f32[256,7168]{1,0:T(8,128)} fusion(f32[256,7168]{1,0:T(8,128)} %fusion.63, bf16[256,256]{0,1:T(8,128)(2,1)S(1)} %get-tuple-element.35, bf16[7168,256]{1,0:T(8,128)(2,1)} %bitcast.10), kind=kOutput, calls=%fused_computation.3 | convolution fusion | flops 941359104 | bytes 18481152 | tf_op jit(solution)/shard_map/rh,dh->rd/dot_general | solution.py:44
  273.9 9.7 %reshape.242 = f32[8,16,2,7168]{3,2,1,0:T(2,128)} reshape(f32[256,7168]{1,0:T(8,128)} %convolution_add_fusion) | data formatting | bytes 14680064 | tf_op jit(solution)/shard_map/reshape | solution.py:52
  283.6 8.3 %copy.88 = f32[8,16,2,7168]{3,1,2,0:T(8,128)} copy(f32[8,16,2,7168]{3,2,1,0:T(2,128)} %reshape.242) | data formatting | bytes 14680064 | tf_op jit(solution)/shard_map/reshape | solution.py:52
  291.9 8.5 %copy.95 = bf16[256,16,448]{0,1,2:T(8,128)(2,1)} copy(bf16[256,16,448]{2,1,0:T(8,128)(2,1)} %reshape.236) | data formatting | bytes 7340032 | tf_op jit(solution)/shard_map/reshape | solution.py:28
  300.4 7.9 %all-to-all-start.8 = ((f32[1,16,2]{2,0,1:T(1,128)}), f32[1,16,2]{2,0,1:T(1,128)S(1)}, u32[]{:S(2)}, u32[]{:S(2)}) async-start(f32[1,16,2]{2,0,1:T(1,128)} %bitcast.81), calls=%async_computation.10 | async-start | bytes 16384 | tf_op jit(solution)/shard_map/all_to_all | solution.py:134
  314.8 7.3 %all-to-all-start.11 = ((bf16[16,256,448]{1,2,0:T(8,128)(2,1)}), bf16[16,256,448]{1,2,0:T(8,128)(2,1)}, u32[]{:S(2)}, u32[]{:S(2)}) async-start(bf16[16,256,448]{1,2,0:T(8,128)(2,1)} %copy.96), calls=%async_computation.13 | async-start | bytes 7340032 | tf_op jit(solution)/shard_map/all_to_all | solution.py:155
  327.2 41.6 %all-to-all-done.11 = bf16[16,256,448]{1,2,0:T(8,128)(2,1)} async-done(((bf16[16,256,448]{1,2,0:T(8,128)(2,1)}), bf16[16,256,448]{1,2,0:T(8,128)(2,1)}, u32[]{:S(2)}, u32[]{:S(2)}) %all-to-all-start.11) | async-done | bytes 3670048 | tf_op jit(solution)/shard_map/all_to_all | solution.py:155
  368.8 9.9 %all-to-all-start.9 = ((bf16[16,448,256]{2,1,0:T(8,128)(2,1)}), bf16[16,448,256]{2,1,0:T(8,128)(2,1)}, u32[]{:S(2)}, u32[]{:S(2)}) async-start(bf16[16,448,256]{2,1,0:T(8,128)(2,1)} %bitcast.77), calls=%async_computation.11 | async-start | bytes 7340032 | tf_op jit(solution)/shard_map/all_to_all | solution.py:153
  383.8 39.6 %all-to-all-done.9 = bf16[16,448,256]{2,1,0:T(8,128)(2,1)} async-done(((bf16[16,448,256]{2,1,0:T(8,128)(2,1)}), bf16[16,448,256]{2,1,0:T(8,128)(2,1)}, u32[]{:S(2)}, u32[]{:S(2)}) %all-to-all-start.9) | async-done | bytes 3670048 | tf_op jit(solution)/shard_map/all_to_all | solution.py:153
  423.4 8.4 %all-to-all-start.10 = ((bf16[16,448,256]{2,1,0:T(8,128)(2,1)}), bf16[16,448,256]{2,1,0:T(8,128)(2,1)}, u32[]{:S(2)}, u32[]{:S(2)}) async-start(bf16[16,448,256]{2,1,0:T(8,128)(2,1)} %bitcast.76), calls=%async_computation.12 | async-start | bytes 7340032 | tf_op jit(solution)/shard_map/all_to_all | solution.py:154
  437.9 40.2 %all-to-all-done.10 = bf16[16,448,256]{2,1,0:T(8,128)(2,1)} async-done(((bf16[16,448,256]{2,1,0:T(8,128)(2,1)}), bf16[16,448,256]{2,1,0:T(8,128)(2,1)}, u32[]{:S(2)}, u32[]{:S(2)}) %all-to-all-start.10) | async-done | bytes 3670048 | tf_op jit(solution)/shard_map/all_to_all | solution.py:154
  478.0 9.0 %all-to-all-start.7 = ((f32[1,16,2,7168]{3,2,0,1:T(2,128)}), f32[1,16,2,7168]{3,2,0,1:T(2,128)S(1)}, u32[]{:S(2)}, u32[]{:S(2)}) async-start(f32[1,16,2,7168]{3,2,0,1:T(2,128)} %copy.89), calls=%async_computation.8 | async-start | bytes 1835008 | tf_op jit(solution)/shard_map/all_to_all | solution.py:133
  506.0 8.5 %convolution_convert_fusion.2 = bf16[256,7168]{1,0:T(8,128)(2,1)} fusion(f32[32,256]{1,0:T(8,128)S(1)} %convert_reduce_fusion, f32[32,7168]{1,0:T(8,128)} %reshape.243), kind=kOutput, calls=%fused_computation.6 | convolution fusion | flops 706478080 | bytes 4620288 | tf_op jit(solution)/shard_map/qt,qd->td/dot_general | solution.py:136
  (105 shorter events, 116.0 us)
Async XLA Ops:
  7.2 55.5 %copy-start = (bf16[8,448,256]{2,1,0:T(8,128)(2,1)S(1)}, bf16[8,448,256]{2,1,0:T(8,128)(2,1)}, u32[]{:S(2)}) copy-start(bf16[8,448,256]{2,1,0:T(8,128)(2,1)} %param.16) | copy-start | bytes 5505028
  7.2 199.4 %all-gather.7.cloned.1.call-start = ((), (), s32[]{:S(2)}) async-start(), calls=%async_computation.17 | async-start | bytes 4128768 | tf_op jit(solution)/shard_map/all_gather | solution.py:119
  23.9 21.2 %copy-start.6 = (bf16[256,8]{0,1:T(8,128)(2,1)S(1)}, bf16[256,8]{0,1:T(8,128)(2,1)}, u32[]{:S(2)}) copy-start(bf16[256,8]{0,1:T(8,128)(2,1)} %param.12) | copy-start | bytes 12292
  24.0 26.9 %copy-start.5 = (s32[256,2]{0,1:T(2,128)S(1)}, s32[256,2]{0,1:T(2,128)}, u32[]{:S(2)}) copy-start(s32[256,2]{0,1:T(2,128)} %param.14) | copy-start | bytes 6148
  46.2 10.9 %all-to-all-start = ((bf16[16,1,2]{2,1,0:T(2,128)(2,1)}), bf16[16,1,2]{2,1,0:T(2,128)(2,1)S(1)}, u32[]{:S(2)}, u32[]{:S(2)}) async-start(bf16[16,1,2]{2,1,0:T(2,128)(2,1)} %all_to_all.52), calls=%async_computation | async-start | bytes 16384 | tf_op jit(solution)/shard_map/all_to_all | solution.py:115
  57.8 12.6 %all-to-all-start.1 = ((bf16[8,1,16,2]{2,3,1,0:T(2,128)(2,1)}), bf16[8,1,16,2]{2,3,1,0:T(2,128)(2,1)S(1)}, u32[]{:S(2)}, u32[]{:S(2)}) async-start(bf16[8,1,16,2]{2,3,1,0:T(2,128)(2,1)} %stack.3), calls=%async_computation.1 | async-start | bytes 8192 | tf_op jit(solution)/shard_map/all_to_all | solution.py:14
  70.4 14.9 %all-to-all-start.2 = ((bf16[16,2,7168]{2,1,0:T(2,128)(2,1)}), bf16[16,2,7168]{2,1,0:T(2,128)(2,1)S(1)}, u32[]{:S(2)}, u32[]{:S(2)}) async-start(bf16[16,2,7168]{2,1,0:T(2,128)(2,1)} %reshape.235), calls=%async_computation.2 | async-start | bytes 917504 | tf_op jit(solution)/shard_map/all_to_all | solution.py:114
  85.3 0.8 copy-start.4
  86.1 55.1 %all-to-all-start.6 = ((bf16[16,448,256]{2,1,0:T(8,128)(2,1)}), bf16[16,448,256]{2,1,0:T(8,128)(2,1)}, u32[]{:S(2)}, u32[]{:S(2)}) async-start(bf16[16,448,256]{2,1,0:T(8,128)(2,1)} %get-tuple-element.39), calls=%async_computation.6 | async-start | bytes 7340032 | tf_op jit(solution)/shard_map/all_to_all | solution.py:106
  91.8 123.2 %all-gather.5.cloned.1.call-start = ((), (), s32[]{:S(2)}) async-start(), calls=%async_computation.16 | async-start | bytes 4128768 | tf_op jit(solution)/shard_map/all_gather | solution.py:120
  141.1 9.1 %copy-start.3 = (bf16[8,256,448]{1,2,0:T(8,128)(2,1)S(1)}, bf16[8,256,448]{1,2,0:T(8,128)(2,1)}, u32[]{:S(2)}) copy-start(bf16[8,256,448]{1,2,0:T(8,128)(2,1)} %param.17) | copy-start | bytes 5505028
  141.1 55.3 %all-to-all-start.5 = ((bf16[16,448,256]{2,1,0:T(8,128)(2,1)}), bf16[16,448,256]{2,1,0:T(8,128)(2,1)}, u32[]{:S(2)}, u32[]{:S(2)}) async-start(bf16[16,448,256]{2,1,0:T(8,128)(2,1)} %get-tuple-element.38), calls=%async_computation.5 | async-start | bytes 7340032 | tf_op jit(solution)/shard_map/all_to_all | solution.py:107
  196.4 53.7 %all-to-all-start.3 = ((bf16[16,256,448]{1,2,0:T(8,128)(2,1)}), bf16[16,256,448]{1,2,0:T(8,128)(2,1)}, u32[]{:S(2)}, u32[]{:S(2)}) async-start(bf16[16,256,448]{1,2,0:T(8,128)(2,1)} %broadcast_select_fusion.2), calls=%async_computation.3 | async-start | bytes 7340032 | tf_op jit(solution)/shard_map/all_to_all | solution.py:108
  206.1 94.3 %reduce-scatter.5.cloned.1.call-start = ((), (), s32[]{:S(2)}) async-start(), calls=%async_computation.15 | async-start | bytes 73728 | tf_op jit(solution)/shard_map/reduce_scatter | solution.py:130
  224.6 4.8 copy-start.2
  265.5 169.6 %reduce-scatter.3.cloned.1.call-start = ((), (), s32[]{:S(2)}) async-start(), calls=%async_computation.14 | async-start | bytes 8257536 | tf_op jit(solution)/shard_map/reduce_scatter | solution.py:129
  300.4 14.4 %all-to-all-start.8 = ((f32[1,16,2]{2,0,1:T(1,128)}), f32[1,16,2]{2,0,1:T(1,128)S(1)}, u32[]{:S(2)}, u32[]{:S(2)}) async-start(f32[1,16,2]{2,0,1:T(1,128)} %bitcast.81), calls=%async_computation.10 | async-start | bytes 16384 | tf_op jit(solution)/shard_map/all_to_all | solution.py:134
  314.8 54.0 %all-to-all-start.11 = ((bf16[16,256,448]{1,2,0:T(8,128)(2,1)}), bf16[16,256,448]{1,2,0:T(8,128)(2,1)}, u32[]{:S(2)}, u32[]{:S(2)}) async-start(bf16[16,256,448]{1,2,0:T(8,128)(2,1)} %copy.96), calls=%async_computation.13 | async-start | bytes 7340032 | tf_op jit(solution)/shard_map/all_to_all | solution.py:155
  368.8 54.6 %all-to-all-start.9 = ((bf16[16,448,256]{2,1,0:T(8,128)(2,1)}), bf16[16,448,256]{2,1,0:T(8,128)(2,1)}, u32[]{:S(2)}, u32[]{:S(2)}) async-start(bf16[16,448,256]{2,1,0:T(8,128)(2,1)} %bitcast.77), calls=%async_computation.11 | async-start | bytes 7340032 | tf_op jit(solution)/shard_map/all_to_all | solution.py:153
  423.4 54.7 %all-to-all-start.10 = ((bf16[16,448,256]{2,1,0:T(8,128)(2,1)}), bf16[16,448,256]{2,1,0:T(8,128)(2,1)}, u32[]{:S(2)}, u32[]{:S(2)}) async-start(bf16[16,448,256]{2,1,0:T(8,128)(2,1)} %bitcast.76), calls=%async_computation.12 | async-start | bytes 7340032 | tf_op jit(solution)/shard_map/all_to_all | solution.py:154
  478.0 26.4 %all-to-all-start.7 = ((f32[1,16,2,7168]{3,2,0,1:T(2,128)}), f32[1,16,2,7168]{3,2,0,1:T(2,128)S(1)}, u32[]{:S(2)}, u32[]{:S(2)}) async-start(f32[1,16,2,7168]{3,2,0,1:T(2,128)} %copy.89), calls=%async_computation.8 | async-start | bytes 1835008 | tf_op jit(solution)/shard_map/all_to_all | solution.py:133
  502.9 11.7 %copy-start.1 = (bf16[8,448,256]{2,1,0:T(8,128)(2,1)S(1)}, bf16[8,448,256]{2,1,0:T(8,128)(2,1)}, u32[]{:S(2)}) copy-start(bf16[8,448,256]{2,1,0:T(8,128)(2,1)} %param.16) | copy-start | bytes 5505028
Sparse Core Ops, SparseCore 0:
  45.1 26.5 all-gather.6
  94.9 29.2 all-gather.4
  265.6 29.2 reduce-scatter.4
  297.1 47.3 reduce-scatter.2
